TPU v7x, 128 devices: a whole 4x4x4 slice. The times are simulated.
128 devices in a mesh: req: 16 (over z, x), exp: 8 (over y, core).
Axes of the slice: x: 4, y: 4, z: 4, core: 2. Of those that a mesh axis runs over, the one named last changes fastest.
Arguments:
- tokens: bfloat16 [12288, 2880], P(('req', 'exp')), may hold values from -6 to 6
- attn_gain: float32 [2880], replicated, may hold values from 0.5 to 8
- w_query: bfloat16 [2880, 4096], P(None, 'exp'), may hold values from -0.109375 to 0.109375
- key_weight: bfloat16 [2880, 512], P(None, 'exp'), may hold values from -0.109375 to 0.109375
- value_weight: bfloat16 [2880, 512], P(None, 'exp'), may hold values from -0.109375 to 0.109375
- sinks: float32 [64], P('exp'), may hold values from -1 to 3
- w_out: bfloat16 [4096, 2880], P('exp'), may hold values from -0.09375 to 0.09375
- ffn_gain: float32 [2880], replicated, may hold values from 0.25 to 1.75
- router: bfloat16 [2880, 32], replicated, may hold values from -0.109375 to 0.109375
- routes: int32 [12288, 4], P(('req', 'exp')), may hold values from 0 to 31, all different within a row; in each aligned block of 96 rows (0 to 95, 96 to 191, ...) at most 14 rows name the same one
- lengths: int32 [16, 6], P('req'), may hold values from 1 to 384, 768 in all within a row
- expert_gate: bfloat16 [128, 2880, 720], P(('req', 'exp')), may hold values from -0.109375 to 0.109375
- expert_up: bfloat16 [128, 2880, 720], P(('req', 'exp')), may hold values from -0.109375 to 0.109375
- expert_down: bfloat16 [128, 720, 2880], P(('req', 'exp')), may hold values from -0.109375 to 0.109375
Outputs:
- layer_out: bfloat16 [12288, 2880], P(('req', 'exp'))
Inputs may be any that keep to these rules, and one draw needn't show every extreme that they name: `routes`: in the rows of one device no expert is named by more than 14 rows, a bound that some block reaches; a row names 4 different experts.
All inputs are finite; a program needn't handle non-finite values.
Results may differ from a plain program's by a relative error of at most 0.02.
The roundings to bfloat16 on the way count: a program that leaves them out, or rounds other values in their place, can miss the bound.
Values may be sent and summed in bfloat16 or wider, within the bound.
No kernel may reach another device: no remote copies, remote signals or barrier semaphores. Data moves between devices by JAX's collectives and lax.ppermute only.
A program may use at most 192 MiB of HBM per device.

v0:
```python
import jax
import jax.numpy as jnp
from jax import lax
from jax.sharding import PartitionSpec as P

QUERY_HEADS = 64
KEY_VALUE_HEADS = 8
HEAD_DIM = 64
EXPERTS = 32
TOPK = 4
CAP = 14


def rms_norm(value_rows, gain):
    mean_sq = jnp.mean(value_rows * value_rows, axis=-1, keepdims=True)
    return value_rows * lax.rsqrt(mean_sq + 1e-05) * gain


def rotate(value_rows, offset):
    half = value_rows.shape[-1] // 2
    freqs = jnp.exp(
        -(2.0 * jnp.arange(half, dtype=jnp.float32) / value_rows.shape[-1])
        * jnp.log(jnp.float32(150000.0))
    )
    angle = offset.astype(jnp.float32)[:, None] * freqs[None, :]
    cosine = jnp.cos(angle)[:, None, :]
    sine = jnp.sin(angle)[:, None, :]
    first = value_rows[..., :half]
    second = value_rows[..., half:]
    return jnp.concatenate(
        [first * cosine - second * sine, second * cosine + first * sine], axis=-1
    )


def per_device(
    tokens,
    attn_gain,
    w_query,
    key_weight,
    value_weight,
    sinks,
    w_out,
    ffn_gain,
    router,
    routes,
    lengths,
    expert_gate,
    expert_up,
    expert_down,
):
    tok_rows = tokens.shape[0]
    model_width = tokens.shape[1]
    local_heads = w_query.shape[1] // HEAD_DIM
    local_kv = key_weight.shape[1] // HEAD_DIM
    head_group = QUERY_HEADS // KEY_VALUE_HEADS
    normed_input = rms_norm(tokens.astype(jnp.float32), attn_gain).astype(jnp.bfloat16)
    piece = lax.all_gather(normed_input, "exp", axis=0, tiled=True)
    projected = jnp.concatenate(
        [
            jnp.dot(piece, w_query, preferred_element_type=jnp.float32),
            jnp.dot(piece, key_weight, preferred_element_type=jnp.float32),
            jnp.dot(piece, value_weight, preferred_element_type=jnp.float32),
        ],
        axis=1,
    )
    item_count = projected.shape[0]
    lens = lengths[0]
    ends = jnp.cumsum(lens)
    starts = ends - lens
    position = jnp.arange(item_count, dtype=jnp.int32)
    member = ((position[:, None] >= starts[None, :]) & (position[:, None] < ends[None, :])).astype(
        jnp.int32
    )
    segment = jnp.sum(member * jnp.arange(lens.shape[0], dtype=jnp.int32)[None, :], axis=1)
    offset = position - jnp.sum(member * starts[None, :], axis=1)
    q_width = local_heads * HEAD_DIM
    kv_width = local_kv * HEAD_DIM
    query_rows = rotate(
        projected[:, :q_width].reshape(item_count, local_heads, HEAD_DIM), offset
    ).astype(jnp.bfloat16)
    key_rows = rotate(
        projected[:, q_width : q_width + kv_width].reshape(item_count, local_kv, HEAD_DIM), offset
    ).astype(jnp.bfloat16)
    value_rows = (
        projected[:, q_width + kv_width :]
        .reshape(item_count, local_kv, HEAD_DIM)
        .astype(jnp.bfloat16)
    )
    grouped_heads = query_rows.reshape(item_count, local_kv, head_group, HEAD_DIM)
    scores = jnp.einsum(
        "qcgd,kcd->cgqk", grouped_heads, key_rows, preferred_element_type=jnp.float32
    ) * HEAD_DIM ** (-0.5)
    allowed = (segment[:, None] == segment[None, :]) & (position[None, :] <= position[:, None])
    sink_score_logit = sinks.reshape(local_kv, head_group, 1, 1)
    masked = jnp.where(allowed[None, None], scores, -jnp.inf)
    top = jnp.maximum(jnp.max(masked, axis=-1, keepdims=True), sink_score_logit)
    expo = jnp.where(allowed[None, None], jnp.exp(scores - top), 0.0)
    denom = jnp.sum(expo, axis=-1, keepdims=True) + jnp.exp(sink_score_logit - top)
    probs = (expo / denom).astype(jnp.bfloat16)
    attended = jnp.einsum("cgqk,kcd->qcgd", probs, value_rows, preferred_element_type=jnp.float32)
    attended = attended.reshape(item_count, q_width).astype(jnp.bfloat16)
    attn_sum = lax.psum_scatter(
        jnp.dot(attended, w_out, preferred_element_type=jnp.float32).astype(jnp.bfloat16),
        "exp",
        scatter_dimension=0,
        tiled=True,
    ).astype(jnp.float32)
    residual = (tokens.astype(jnp.float32) + attn_sum).astype(jnp.bfloat16)
    normed2 = rms_norm(residual.astype(jnp.float32), ffn_gain).astype(jnp.bfloat16)
    logits = jnp.dot(normed2, router, preferred_element_type=jnp.float32)
    picked = jnp.take_along_axis(logits, routes, axis=1)
    weights = jax.nn.softmax(picked, axis=-1)
    flat_routes = routes.reshape(-1)
    expert_ids = jnp.arange(EXPERTS, dtype=jnp.int32)
    onehot_route = (flat_routes[:, None] == expert_ids[None, :]).astype(jnp.int32)
    rank = jnp.cumsum(onehot_route, axis=0) - 1
    slot_rank = jnp.sum(onehot_route * rank, axis=1)
    flat_slot = flat_routes * CAP + slot_rank
    slot_ids = jnp.arange(EXPERTS * CAP, dtype=jnp.int32)
    dispatch_table = (slot_ids[:, None] == flat_slot[None, :]).astype(jnp.bfloat16)
    repeated = jnp.repeat(normed2, TOPK, axis=0)
    packed = jnp.dot(dispatch_table, repeated, preferred_element_type=jnp.float32).astype(
        jnp.bfloat16
    )
    n_req = lax.axis_size("req")
    n_exp = lax.axis_size("exp")
    devices = n_req * n_exp
    split = devices // EXPERTS
    send_rows = jnp.broadcast_to(
        packed.reshape(EXPERTS, 1, CAP, model_width), (EXPERTS, split, CAP, model_width)
    ).reshape(devices, CAP, model_width)
    received = lax.all_to_all(send_rows, ("req", "exp"), split_axis=0, concat_axis=0, tiled=True)
    flat_rows = received.reshape(-1, model_width)
    gate = jnp.dot(flat_rows, expert_gate[0], preferred_element_type=jnp.float32)
    up_val = jnp.dot(flat_rows, expert_up[0], preferred_element_type=jnp.float32)
    hidden = ((up_val + 1.0) * gate * jax.nn.sigmoid(1.702 * gate)).astype(jnp.bfloat16)
    slice_out = jnp.dot(hidden, expert_down[0], preferred_element_type=jnp.float32).astype(
        jnp.bfloat16
    )
    returned = lax.all_to_all(
        slice_out.reshape(received.shape), ("req", "exp"), split_axis=0, concat_axis=0, tiled=True
    )
    summed = returned.astype(jnp.float32).reshape(EXPERTS, split, CAP, model_width).sum(axis=1)
    summed = summed.reshape(EXPERTS * CAP, model_width)
    picked_rows = jnp.take(summed, flat_slot, axis=0).reshape(tok_rows, TOPK, model_width)
    moe_sum = jnp.sum(weights[:, :, None] * picked_rows, axis=1)
    return (residual.astype(jnp.float32) + moe_sum).astype(jnp.bfloat16)


def solution(mesh):
    return jax.shard_map(
        per_device,
        mesh=mesh,
        in_specs=(
            P(("req", "exp"), None),
            P(),
            P(None, "exp"),
            P(None, "exp"),
            P(None, "exp"),
            P("exp"),
            P("exp", None),
            P(),
            P(),
            P(("req", "exp"), None),
            P("req", None),
            P(("req", "exp"), None, None),
            P(("req", "exp"), None, None),
            P(("req", "exp"), None, None),
        ),
        out_specs=P(("req", "exp"), None),
        check_vma=False,
    )
```

profile of v0, /device:TPU:14, one launch (start us, length us, event | category | flops | bytes accessed | tf_op | source)
XLA Modules:
  0.0 587.9 jit_solution(4064006883043466249)
XLA Ops:
  13.2 31.8 %all-gather.2.cloned.1.call-done = bf16[768,2880]{1,0:T(8,128)(2,1)} async-done(((bf16[96,2880]{1,0:T(8,128)(2,1)}), bf16[768,2880]{1,0:T(8,128)(2,1)}) %all-gather.2.cloned.1.call-update) | async-done | bytes 4423696 | tf_op jit(solution)/shard_map/all_gather | solution.py:57
  45.0 3.9 convolution_bitcast_fusion
  49.4 4.6 fusion.59
  54.2 8.6 %fusion = (f32[8,768]{1,0:T(8,128)S(1)}, f32[768,768,8]{1,0,2:T(8,128)}) fusion(pred[768,768]{0,1:T(8,128)(4,1)S(1)} %fusion.13, bf16[768,8,32]{0,2,1:T(8,128)(2,1)S(1)} %get-tuple-element.10, bf16[768,8,32]{0,2,1:T(8,128)(2,1)S(1)} %get-tuple-element.9, bf16[768,32]{0,1:T(8,128)(2,1)S(1)} %get-tuple-element.12, bf16[768,32]{0,1:T(8,128)(2,1)S(1)} %get-tuple-element.11), kind=kOutput, calls=%fused_computation.5 | convolution fusion | flops 619898880 | bytes 20373504 | tf_op jit(solution)/shard_map/qcgd,kcd->cgqk/dot_general | solution.py:90
  64.2 10.8 %fusion.3 = f32[8,768]{1,0:T(8,128)} fusion(f32[768,768,8]{1,0,2:T(8,128)} %get-tuple-element.16, f32[8,768]{1,0:T(8,128)} %broadcast_maximum_fusion, pred[768,768]{0,1:T(8,128)(4,1)S(1)} %fusion.13), kind=kLoop, calls=%fused_computation.9 | loop fusion | flops 18868224 | bytes 19513344 | tf_op jit(solution)/shard_map/reduce_sum | solution.py:98
  76.4 14.1 %fusion.16 = bf16[64,8,768]{2,0,1:T(8,128)(2,1)} fusion(f32[8,768]{1,0:T(8,128)} %exponential_add_fusion, f32[8,768]{1,0:T(8,128)} %broadcast_maximum_fusion, f32[768,768,8]{1,0,2:T(8,128)} %get-tuple-element.16, pred[768,768]{0,1:T(8,128)(4,1)S(1)} %fusion.13, bf16[768,2880]{1,0:T(8,128)(2,1)} %all-gather.2.cloned.1.call-done, bf16[2880,64]{0,1:T(8,128)(2,1)} %param.18), kind=kOutput, calls=%fused_computation.30 | convolution fusion | flops 911130624 | bytes 25092096 | tf_op jit(solution)/shard_map/cgqk,kcd->qcgd/dot_general | solution.py:100
  90.5 5.8 convolution_convert_fusion.1
  98.7 33.6 %reduce-scatter.2.cloned.1.call-done = bf16[96,2880]{1,0:T(8,128)(2,1)} async-done(((bf16[768,2880]{1,0:T(8,128)(2,1)}), bf16[96,2880]{1,0:T(8,128)(2,1)}) %reduce-scatter.2.cloned.1.call-update) | async-done | bytes 552976 | tf_op jit(solution)/shard_map/reduce_scatter | solution.py:102
  138.1 4.7 convolution_convert_fusion.2
  142.8 4.4 broadcast_in_dim.41
  147.2 7.1 %broadcast_in_dim.42 = bf16[32,4,14,2880]{3,2,1,0:T(8,128)(2,1)} broadcast(bf16[32,14,2880]{2,1,0:T(8,128)(2,1)} %broadcast_in_dim.41), dimensions={0,2,3} | broadcast | bytes 12902400 | tf_op jit(solution)/shard_map/broadcast_in_dim | solution.py:129
  154.3 146.0 %all_to_all.10 = bf16[128,14,2880]{2,1,0:T(8,128)(2,1)} all-to-all(bf16[128,14,2880]{2,1,0:T(8,128)(2,1)} %bitcast.104), channel_id=1, replica_groups=mesh['req'=16,'exp'=8] {'req','exp'}, dimensions={0} | all-to-all | bytes 20643840 | tf_op jit(solution)/shard_map/all_to_all | solution.py:132
  300.4 15.4 %reshape.419 = bf16[1792,2880]{1,0:T(8,128)(2,1)} reshape(bf16[128,14,2880]{2,1,0:T(8,128)(2,1)} %all_to_all.10) | data formatting | bytes 20643840 | tf_op jit(solution)/shard_map/reshape | solution.py:133
  315.7 14.6 %fusion.7 = f32[1792,720]{0,1:T(8,128)} fusion(bf16[1792,2880]{1,0:T(8,128)(2,1)} %reshape.419, bf16[1,2880,720]{1,2,0:T(8,128)(2,1)} %param.25), kind=kOutput, calls=%fused_computation.18 | convolution fusion | flops 7431782400 | bytes 19630080 | tf_op jit(solution)/shard_map/dot_general | solution.py:134
  330.3 27.2 %convolution_convert_fusion = bf16[1792,2880]{0,1:T(8,128)(2,1)} fusion(bf16[1,720,2880]{2,1,0:T(8,128)(2,1)} %param.27, f32[1792,720]{0,1:T(8,128)} %fusion.7, bf16[1792,2880]{1,0:T(8,128)(2,1)} %reshape.419, bf16[1,2880,720]{1,2,0:T(8,128)(2,1)} %param.26), kind=kOutput, calls=%fused_computation.10 | convolution fusion | flops 14879047680 | bytes 34099200 | tf_op jit(solution)/shard_map/dot_general | solution.py:137
  357.6 14.3 %copy.49 = bf16[1792,2880]{1,0:T(8,128)(2,1)} copy(bf16[1792,2880]{0,1:T(8,128)(2,1)} %convolution_convert_fusion) | data formatting | bytes 20643840 | tf_op jit(solution)/shard_map/convert_element_type | solution.py:137
  371.9 14.4 %reshape.420 = bf16[128,14,2880]{2,1,0:T(8,128)(2,1)} reshape(bf16[1792,2880]{1,0:T(8,128)(2,1)} %copy.49) | data formatting | bytes 20643840 | tf_op jit(solution)/shard_map/reshape | solution.py:141
  386.3 8.2 %all-to-all-start.1 = ((bf16[128,14,2880]{2,1,0:T(8,128)(2,1)}), bf16[128,14,2880]{2,1,0:T(8,128)(2,1)}, u32[]{:S(2)}, u32[]{:S(2)}) async-start(bf16[128,14,2880]{2,1,0:T(8,128)(2,1)} %reshape.420), calls=%async_computation.2 | async-start | bytes 24117248 | tf_op jit(solution)/shard_map/all_to_all | solution.py:140
  399.5 143.8 %all-to-all-done.1 = bf16[128,14,2880]{2,1,0:T(8,128)(2,1)} async-done(((bf16[128,14,2880]{2,1,0:T(8,128)(2,1)}), bf16[128,14,2880]{2,1,0:T(8,128)(2,1)}, u32[]{:S(2)}, u32[]{:S(2)}) %all-to-all-start.1) | async-done | bytes 10321952 | tf_op jit(solution)/shard_map/all_to_all | solution.py:140
  543.3 9.8 %convert_reduce_fusion = f32[32,14,2880]{2,1,0:T(8,128)} fusion(bf16[128,14,2880]{2,1,0:T(8,128)(2,1)} %all-to-all-done.1), kind=kLoop, calls=%fused_computation.2 | loop fusion | flops 9031680 | bytes 15482880 | tf_op jit(solution)/shard_map/reduce_sum | solution.py:143
  553.1 5.6 reshape.423
  558.7 9.1 %gather_fusion = f32[384,2880]{1,0:T(8,128)} fusion(f32[448,2880]{1,0:T(8,128)} %reshape.423, s32[1024]{0:T(1024)S(1)} %pad_clamp_fusion), kind=kCustom, calls=%fused_computation | custom fusion | bytes 8848896 | tf_op jit(solution)/shard_map/jit(_take)/gather | solution.py:145
  567.8 5.5 gather.12
  573.3 6.5 %multiply_reduce_fusion = f32[96,2880]{1,0:T(8,128)S(1)} fusion(f32[96,4,2880]{2,1,0:T(4,128)} %gather.12, f32[96,4]{1,0:T(8,128)} %copy.43, pred[96,4]{1,0:T(8,128)(4,1)S(1)} %copy.48), kind=kLoop, calls=%fused_computation.15 | loop fusion | flops 3041280 | bytes 5531520 | tf_op jit(solution)/shard_map/reduce_sum | solution.py:146
  (77 shorter events, 24.0 us)
Async XLA Ops:
  6.5 83.9 %copy-start = (bf16[512,2880]{0,1:T(8,128)(2,1)S(1)}, bf16[512,2880]{0,1:T(8,128)(2,1)}, u32[]{:S(2)}) copy-start(bf16[512,2880]{0,1:T(8,128)(2,1)} %param.20) | copy-start | bytes 8847364
  6.5 38.4 %all-gather.2.cloned.1.call-start = ((), (), s32[]{:S(2)}) async-start(), calls=%async_computation.3 | async-start | bytes 5087232 | tf_op jit(solution)/shard_map/all_gather | solution.py:57
  10.1 122.3 %reduce-scatter.2.cloned.1.call-start = ((), (), s32[]{:S(2)}) async-start(), calls=%async_computation.4 | async-start | bytes 5087232 | tf_op jit(solution)/shard_map/reduce_scatter | solution.py:102
  45.0 4.4 copy-start.4
  49.3 4.7 copy-start.5
  49.3 4.7 copy-start.6
  54.2 9.3 %copy-start.11 = (f32[8]{0:T(128)S(1)}, f32[8]{0:T(128)}, u32[]{:S(2)}) copy-start(f32[8]{0:T(128)} %param.19) | copy-start | bytes 100
  62.9 0.6 copy-start.7
  96.3 0.7 copy-start.9
  96.3 36.1 %copy-start.2 = (bf16[96,2880]{1,0:T(8,128)(2,1)S(1)}, bf16[96,2880]{1,0:T(8,128)(2,1)}, u32[]{:S(2)}) copy-start(bf16[96,2880]{1,0:T(8,128)(2,1)} %param.14) | copy-start | bytes 1658884
  96.3 37.4 %copy-start.10 = (f32[2880]{0:T(1024)S(1)}, f32[2880]{0:T(1024)}, u32[]{:S(2)}) copy-start(f32[2880]{0:T(1024)} %param.21) | copy-start | bytes 34564
  386.3 9.0 %copy-start.8 = (bf16[2880,32]{0,1:T(8,128)(2,1)S(1)}, bf16[2880,32]{0,1:T(8,128)(2,1)}, u32[]{:S(2)}) copy-start(bf16[2880,32]{0,1:T(8,128)(2,1)} %param.22) | copy-start | bytes 552964
  386.3 157.0 %all-to-all-start.1 = ((bf16[128,14,2880]{2,1,0:T(8,128)(2,1)}), bf16[128,14,2880]{2,1,0:T(8,128)(2,1)}, u32[]{:S(2)}, u32[]{:S(2)}) async-start(bf16[128,14,2880]{2,1,0:T(8,128)(2,1)} %reshape.420), calls=%async_computation.2 | async-start | bytes 24117248 | tf_op jit(solution)/shard_map/all_to_all | solution.py:140
  567.8 13.1 %copy-start.1 = (bf16[512,2880]{0,1:T(8,128)(2,1)S(1)}, bf16[512,2880]{0,1:T(8,128)(2,1)}, u32[]{:S(2)}) copy-start(bf16[512,2880]{0,1:T(8,128)(2,1)} %param.20) | copy-start | bytes 8847364
  573.3 6.5 %copy-start.3 = (bf16[96,2880]{1,0:T(8,128)(2,1)S(1)}, bf16[96,2880]{1,0:T(8,128)(2,1)}, u32[]{:S(2)}) copy-start(bf16[96,2880]{1,0:T(8,128)(2,1)} %reduce-scatter.2.cloned.1.call-done) | copy-start | bytes 1658884
Sparse Core Ops, SparseCore 0:
  10.2 34.7 all-gather.1
  96.5 35.8 reduce-scatter.1
where the time goes:
time: 594 us; the launch traced here: 588 us
  waiting for transfers between devices  209 us (35%)
  blocking collectives  146 us (25%)
  local copies, waits for them, and re-layouts  85.3 us (14%)
  matrix products  83.9 us (14%)
  other arithmetic  41.3 us (7%)
  between operations  13.9 us (2%)
  starting transfers between devices  8.24 us (1%)
    all_to_all x1, blocking collectives, per_device(): lax.all_to_all(send_rows, ('req', 'exp'), split_axis=0, concat_axis=0, ti...  146 us
    all_to_all x1, waiting for transfers between devices, per_device(): lax.all_to_all(slice_out.reshape(received.shape), ('req', 'exp'), split_a...  144 us
    reduce_scatter x1, waiting for transfers between devices, per_device(): lax.psum_scatter(jnp.dot(attended, w_out, preferred_element_type=jnp.floa...  33.6 us
    all_gather x1, waiting for transfers between devices, per_device(): piece = lax.all_gather(normed_input, 'exp', axis=0, tiled=True)  31.8 us
    dot_general x1, matrix products, per_device(): jnp.dot(hidden, expert_down[0], preferred_element_type=jnp.float32)  27.2 us
    reshape x1, local copies, waits for them, and re-layouts, per_device(): flat_rows = received.reshape(-1, model_width)  15.4 us
    gather x2, local copies, waits for them, and re-layouts, per_device(): jnp.take(summed, flat_slot, axis=0).reshape(tok_rows, TOPK, model_width)  14.6 us
    dot_general x1, matrix products, per_device(): jnp.dot(flat_rows, expert_gate[0], preferred_element_type=jnp.float32)  14.6 us
  transfers between devices with their start and end apart: 3, of which 3 were waited for; matrix products, arithmetic and copies ran while one was open for 2% of the time, Pallas kernels for 0%

commit v1 on v0

--- a/solution.py
+++ b/solution.py
@@ -54,7 +54,11 @@
     local_kv = key_weight.shape[1] // HEAD_DIM
     head_group = QUERY_HEADS // KEY_VALUE_HEADS
     normed_input = rms_norm(tokens.astype(jnp.float32), attn_gain).astype(jnp.bfloat16)
-    piece = lax.all_gather(normed_input, "exp", axis=0, tiled=True)
+    peers = lax.axis_size("exp")
+    repeats = [peers if d == 0 else 1 for d in range(normed_input.ndim)]
+    piece = lax.all_to_all(
+        jnp.tile(normed_input, repeats), "exp", split_axis=0, concat_axis=0, tiled=True
+    )
     projected = jnp.concatenate(
         [
             jnp.dot(piece, w_query, preferred_element_type=jnp.float32),

time: 594 us -> 622 us (1.047)
  waiting for transfers between devices: 209 us -> 223 us
  local copies, waits for them, and re-layouts: 85.3 us -> 92.3 us
    all_to_all x0 -> x1, waiting for transfers between devices: none -> 45.5 us  [per_device(): lax.all_to_all(jnp.tile(normed_input, repeats), 'exp', split_axis=0, conc...]
    all_gather x1 -> x0, waiting for transfers between devices: 31.8 us -> none  [per_device(): piece = lax.all_gather(normed_input, 'exp', axis=0, tiled=True)]
where the time goes in v1:
time: 622 us; the launch traced here: 612 us
  waiting for transfers between devices  223 us (36%)
  blocking collectives  146 us (23%)
  local copies, waits for them, and re-layouts  92.3 us (15%)
  matrix products  84.2 us (14%)
  other arithmetic  39 us (6%)
  between operations  13.9 us (2%)
  starting transfers between devices  13.1 us (2%)
    all_to_all x1, blocking collectives, per_device(): lax.all_to_all(send_rows, ('req', 'exp'), split_axis=0, concat_axis=0, ti...  146 us
    all_to_all x1, waiting for transfers between devices, per_device(): lax.all_to_all(slice_out.reshape(received.shape), ('req', 'exp'), split_a...  144 us
    all_to_all x1, waiting for transfers between devices, per_device(): lax.all_to_all(jnp.tile(normed_input, repeats), 'exp', split_axis=0, conc...  45.5 us
    reduce_scatter x1, waiting for transfers between devices, per_device(): lax.psum_scatter(jnp.dot(attended, w_out, preferred_element_type=jnp.floa...  34.2 us
    dot_general x1, matrix products, per_device(): jnp.dot(hidden, expert_down[0], preferred_element_type=jnp.float32)  27.2 us
    reshape x1, local copies, waits for them, and re-layouts, per_device(): flat_rows = received.reshape(-1, model_width)  15.4 us
    gather x2, local copies, waits for them, and re-layouts, per_device(): jnp.take(summed, flat_slot, axis=0).reshape(tok_rows, TOPK, model_width)  14.6 us
    dot_general x1, matrix products, per_device(): jnp.dot(flat_rows, expert_gate[0], preferred_element_type=jnp.float32)  14.6 us
  transfers between devices with their start and end apart: 3, of which 3 were waited for; matrix products, arithmetic and copies ran while one was open for 2% of the time, Pallas kernels for 0%

profile of v1, /device:TPU:14, one launch (start us, length us, event | category | flops | bytes accessed | tf_op | source)
XLA Modules:
  0.0 612.2 jit_solution(966165134406298358)
XLA Ops:
  11.6 4.9 all-to-all-start
  16.5 4.6 copy.46
  22.9 45.5 %all-to-all-done = bf16[8,96,2880]{2,1,0:T(8,128)(2,1)} async-done(((bf16[8,96,2880]{2,1,0:T(8,128)(2,1)}), bf16[8,96,2880]{2,1,0:T(8,128)(2,1)}, u32[]{:S(2)}, u32[]{:S(2)}) %all-to-all-start) | async-done | bytes 4423712 | tf_op jit(solution)/shard_map/all_to_all | solution.py:59
  72.8 5.0 fusion.59
  78.0 8.2 %fusion = (f32[8,768]{1,0:T(8,128)S(1)}, f32[768,768,8]{1,0,2:T(8,128)}) fusion(pred[768,768]{0,1:T(8,128)(4,1)S(1)} %fusion.13, bf16[768,8,32]{0,2,1:T(8,128)(2,1)S(1)} %get-tuple-element.10, bf16[768,8,32]{0,2,1:T(8,128)(2,1)S(1)} %get-tuple-element.9, bf16[768,32]{0,1:T(8,128)(2,1)S(1)} %get-tuple-element.12, bf16[768,32]{0,1:T(8,128)(2,1)S(1)} %get-tuple-element.11), kind=kOutput, calls=%fused_computation.5 | convolution fusion | flops 619898880 | bytes 20373504 | tf_op jit(solution)/shard_map/qcgd,kcd->cgqk/dot_general | solution.py:94
  87.4 10.8 %fusion.3 = f32[8,768]{1,0:T(8,128)} fusion(f32[768,768,8]{1,0,2:T(8,128)} %get-tuple-element.16, f32[8,768]{1,0:T(8,128)} %broadcast_maximum_fusion, pred[768,768]{0,1:T(8,128)(4,1)S(1)} %fusion.13), kind=kLoop, calls=%fused_computation.9 | loop fusion | flops 18868224 | bytes 19513344 | tf_op jit(solution)/shard_map/reduce_sum | solution.py:102
  99.7 14.5 %fusion.16 = bf16[64,8,768]{2,0,1:T(8,128)(2,1)} fusion(f32[8,768]{1,0:T(8,128)} %exponential_add_fusion, f32[8,768]{1,0:T(8,128)} %broadcast_maximum_fusion, f32[768,768,8]{1,0,2:T(8,128)} %get-tuple-element.16, pred[768,768]{0,1:T(8,128)(4,1)S(1)} %fusion.13, bf16[768,2880]{1,0:T(8,128)(2,1)} %bitcast, bf16[2880,64]{0,1:T(8,128)(2,1)} %param.18), kind=kOutput, calls=%fused_computation.30 | convolution fusion | flops 911130624 | bytes 25092096 | tf_op jit(solution)/shard_map/cgqk,kcd->qcgd/dot_general | solution.py:104
  114.2 5.8 convolution_convert_fusion.1
  122.3 34.2 %reduce-scatter.2.cloned.1.call-done = bf16[96,2880]{1,0:T(8,128)(2,1)} async-done(((bf16[768,2880]{1,0:T(8,128)(2,1)}), bf16[96,2880]{1,0:T(8,128)(2,1)}) %reduce-scatter.2.cloned.1.call-update) | async-done | bytes 552976 | tf_op jit(solution)/shard_map/reduce_scatter | solution.py:106
  162.2 4.7 convolution_convert_fusion.2
  171.3 7.1 %broadcast_in_dim.42 = bf16[32,4,14,2880]{3,2,1,0:T(8,128)(2,1)} broadcast(bf16[32,14,2880]{2,1,0:T(8,128)(2,1)} %broadcast_in_dim.41), dimensions={0,2,3} | broadcast | bytes 12902400 | tf_op jit(solution)/shard_map/broadcast_in_dim | solution.py:133
  178.4 146.2 %all_to_all.19 = bf16[128,14,2880]{2,1,0:T(8,128)(2,1)} all-to-all(bf16[128,14,2880]{2,1,0:T(8,128)(2,1)} %bitcast.109), channel_id=1, replica_groups=mesh['req'=16,'exp'=8] {'req','exp'}, dimensions={0} | all-to-all | bytes 20643840 | tf_op jit(solution)/shard_map/all_to_all | solution.py:136
  324.7 15.4 %reshape.424 = bf16[1792,2880]{1,0:T(8,128)(2,1)} reshape(bf16[128,14,2880]{2,1,0:T(8,128)(2,1)} %all_to_all.19) | data formatting | bytes 20643840 | tf_op jit(solution)/shard_map/reshape | solution.py:137
  340.0 14.6 %fusion.7 = f32[1792,720]{0,1:T(8,128)} fusion(bf16[1792,2880]{1,0:T(8,128)(2,1)} %reshape.424, bf16[1,2880,720]{1,2,0:T(8,128)(2,1)} %param.25), kind=kOutput, calls=%fused_computation.18 | convolution fusion | flops 7431782400 | bytes 19630080 | tf_op jit(solution)/shard_map/dot_general | solution.py:138
  354.6 27.2 %convolution_convert_fusion = bf16[1792,2880]{0,1:T(8,128)(2,1)} fusion(bf16[1,720,2880]{2,1,0:T(8,128)(2,1)} %param.27, f32[1792,720]{0,1:T(8,128)} %fusion.7, bf16[1792,2880]{1,0:T(8,128)(2,1)} %reshape.424, bf16[1,2880,720]{1,2,0:T(8,128)(2,1)} %param.26), kind=kOutput, calls=%fused_computation.10 | convolution fusion | flops 14879047680 | bytes 34099200 | tf_op jit(solution)/shard_map/dot_general | solution.py:141
  381.8 14.3 %copy.57 = bf16[1792,2880]{1,0:T(8,128)(2,1)} copy(bf16[1792,2880]{0,1:T(8,128)(2,1)} %convolution_convert_fusion) | data formatting | bytes 20643840 | tf_op jit(solution)/shard_map/convert_element_type | solution.py:141
  396.2 14.4 %reshape.425 = bf16[128,14,2880]{2,1,0:T(8,128)(2,1)} reshape(bf16[1792,2880]{1,0:T(8,128)(2,1)} %copy.57) | data formatting | bytes 20643840 | tf_op jit(solution)/shard_map/reshape | solution.py:145
  410.6 8.2 %all-to-all-start.2 = ((bf16[128,14,2880]{2,1,0:T(8,128)(2,1)}), bf16[128,14,2880]{2,1,0:T(8,128)(2,1)}, u32[]{:S(2)}, u32[]{:S(2)}) async-start(bf16[128,14,2880]{2,1,0:T(8,128)(2,1)} %reshape.425), calls=%async_computation.3 | async-start | bytes 24117248 | tf_op jit(solution)/shard_map/all_to_all | solution.py:144
  423.8 143.8 %all-to-all-done.2 = bf16[128,14,2880]{2,1,0:T(8,128)(2,1)} async-done(((bf16[128,14,2880]{2,1,0:T(8,128)(2,1)}), bf16[128,14,2880]{2,1,0:T(8,128)(2,1)}, u32[]{:S(2)}, u32[]{:S(2)}) %all-to-all-start.2) | async-done | bytes 10321952 | tf_op jit(solution)/shard_map/all_to_all | solution.py:144
  567.6 9.8 %convert_reduce_fusion = f32[32,14,2880]{2,1,0:T(8,128)} fusion(bf16[128,14,2880]{2,1,0:T(8,128)(2,1)} %all-to-all-done.2), kind=kLoop, calls=%fused_computation.2 | loop fusion | flops 9031680 | bytes 15482880 | tf_op jit(solution)/shard_map/reduce_sum | solution.py:147
  577.4 5.6 reshape.428
  583.0 9.1 %gather_fusion = f32[384,2880]{1,0:T(8,128)} fusion(f32[448,2880]{1,0:T(8,128)} %reshape.428, s32[1024]{0:T(1024)S(1)} %pad_clamp_fusion), kind=kCustom, calls=%fused_computation | custom fusion | bytes 8848896 | tf_op jit(solution)/shard_map/jit(_take)/gather | solution.py:149
  592.1 5.5 gather.12
  597.6 6.5 %multiply_reduce_fusion = f32[96,2880]{1,0:T(8,128)S(1)} fusion(f32[96,4,2880]{2,1,0:T(4,128)} %gather.12, f32[96,4]{1,0:T(8,128)} %copy.51, pred[96,4]{1,0:T(8,128)(4,1)S(1)} %copy.56), kind=kLoop, calls=%fused_computation.15 | loop fusion | flops 3041280 | bytes 5531520 | tf_op jit(solution)/shard_map/reduce_sum | solution.py:150
  (80 shorter events, 32.4 us)
Async XLA Ops:
  6.5 107.7 %copy-start = (bf16[512,2880]{0,1:T(8,128)(2,1)S(1)}, bf16[512,2880]{0,1:T(8,128)(2,1)}, u32[]{:S(2)}) copy-start(bf16[512,2880]{0,1:T(8,128)(2,1)} %param.20) | copy-start | bytes 8847364
  11.6 56.8 %all-to-all-start = ((bf16[8,96,2880]{2,1,0:T(8,128)(2,1)}), bf16[8,96,2880]{2,1,0:T(8,128)(2,1)}, u32[]{:S(2)}, u32[]{:S(2)}) async-start(bf16[8,96,2880]{2,1,0:T(8,128)(2,1)} %tile.2), calls=%async_computation | async-start | bytes 9043968 | tf_op jit(solution)/shard_map/all_to_all | solution.py:59
  16.5 4.6 copy-start.12
  16.5 140.0 %reduce-scatter.2.cloned.1.call-start = ((), (), s32[]{:S(2)}) async-start(), calls=%async_computation.4 | async-start | bytes 5087232 | tf_op jit(solution)/shard_map/reduce_scatter | solution.py:106
  68.4 4.4 copy-start.4
  72.7 5.0 copy-start.5
  72.7 5.0 copy-start.6
  78.0 8.8 %copy-start.11 = (f32[8]{0:T(128)S(1)}, f32[8]{0:T(128)}, u32[]{:S(2)}) copy-start(f32[8]{0:T(128)} %param.19) | copy-start | bytes 100
  86.2 0.6 copy-start.7
  120.0 0.7 copy-start.9
  120.0 36.5 %copy-start.2 = (bf16[96,2880]{1,0:T(8,128)(2,1)S(1)}, bf16[96,2880]{1,0:T(8,128)(2,1)}, u32[]{:S(2)}) copy-start(bf16[96,2880]{1,0:T(8,128)(2,1)} %param.14) | copy-start | bytes 1658884
  120.0 37.8 %copy-start.10 = (f32[2880]{0:T(1024)S(1)}, f32[2880]{0:T(1024)}, u32[]{:S(2)}) copy-start(f32[2880]{0:T(1024)} %param.21) | copy-start | bytes 34564
  410.6 9.0 %copy-start.8 = (bf16[2880,32]{0,1:T(8,128)(2,1)S(1)}, bf16[2880,32]{0,1:T(8,128)(2,1)}, u32[]{:S(2)}) copy-start(bf16[2880,32]{0,1:T(8,128)(2,1)} %param.22) | copy-start | bytes 552964
  410.6 157.0 %all-to-all-start.2 = ((bf16[128,14,2880]{2,1,0:T(8,128)(2,1)}), bf16[128,14,2880]{2,1,0:T(8,128)(2,1)}, u32[]{:S(2)}, u32[]{:S(2)}) async-start(bf16[128,14,2880]{2,1,0:T(8,128)(2,1)} %reshape.425), calls=%async_computation.3 | async-start | bytes 24117248 | tf_op jit(solution)/shard_map/all_to_all | solution.py:144
  592.1 13.1 %copy-start.1 = (bf16[512,2880]{0,1:T(8,128)(2,1)S(1)}, bf16[512,2880]{0,1:T(8,128)(2,1)}, u32[]{:S(2)}) copy-start(bf16[512,2880]{0,1:T(8,128)(2,1)} %param.20) | copy-start | bytes 8847364
  597.6 6.5 %copy-start.3 = (bf16[96,2880]{1,0:T(8,128)(2,1)S(1)}, bf16[96,2880]{1,0:T(8,128)(2,1)}, u32[]{:S(2)}) copy-start(bf16[96,2880]{1,0:T(8,128)(2,1)} %reduce-scatter.2.cloned.1.call-done) | copy-start | bytes 1658884
Sparse Core Ops, SparseCore 0:
  120.2 36.2 reduce-scatter.1
